TPU v7x, 256 devices: a whole 4x4x8 slice. The times are simulated.
256 devices in a mesh: dp: 32 (over z, y), tensor: 8 (over x, core).
Axes of the slice: x: 4, y: 4, z: 8, core: 2. Of those that a mesh axis runs over, the one named last changes fastest.
Arguments:
- tokens: bfloat16 [4096, 4096], P('dp', 'tensor'), may hold values from -6 to 6
- grad_out: bfloat16 [4096, 4096], P('dp', 'tensor'), may hold values from -6 to 6
- gate_blocks: int32 [8, 32], P('tensor'), may hold values from -1 to 447, as said below
- gate_values: bfloat16 [8, 32, 128, 128], P('tensor'), may hold values from -0.375 to 0.375
- up_blocks: int32 [8, 32], P('tensor'), may hold values from -1 to 447, as said below
- up_values: bfloat16 [8, 32, 128, 128], P('tensor'), may hold values from -0.375 to 0.375
- down_blocks: int32 [8, 32], P('tensor'), may hold values from -1 to 447, as said below
- down_values: bfloat16 [8, 32, 128, 128], P('tensor'), may hold values from -0.1875 to 0.1875
Outputs:
- mixed: bfloat16 [4096, 4096], P('dp', 'tensor')
- grad_tokens: bfloat16 [4096, 4096], P('dp', 'tensor')
- grad_gate: float32 [8, 32, 128, 128], P('tensor', 'dp')
- grad_up: float32 [8, 32, 128, 128], P('tensor', 'dp')
- grad_down: float32 [8, 32, 128, 128], P('tensor', 'dp')
Inputs may be any that keep to these rules, and one draw needn't show every extreme that they name: `gate_blocks`: each row lists distinct block numbers of one tensor shard in its first slots and -1 in the rest; a row has 16 to 32 listed blocks, one row has exactly 32 and another exactly 16. `up_blocks`: as for gate_blocks, drawn apart. `down_blocks`: as for gate_blocks, drawn apart.
All inputs are finite; a program needn't handle non-finite values.
Results may differ from a plain program's by a relative error of at most 0.015.
Values may be sent and summed in bfloat16 or wider, within the bound.
No kernel may reach another device: no remote copies, remote signals or barrier semaphores. Data moves between devices by JAX's collectives and lax.ppermute only.
A program may use at most 64 MiB of HBM per device.

v0:
```python
import jax
import jax.numpy as jnp
from jax import lax
from jax.sharding import PartitionSpec as P

FF = 14336


def locate(blocks, feature_count):
    flat = blocks[0]
    weight = (flat >= 0).astype(jnp.float32)
    safe = jnp.maximum(flat, 0)
    return (safe // feature_count, safe % feature_count, weight)


def one_hot(targets, weight, count):
    return (targets[:, None] == jnp.arange(count)[None, :]).astype(jnp.float32) * weight[:, None]


def spread(product, table):
    return jnp.einsum("tsn,sc->tcn", product, table, precision=lax.Precision.HIGHEST)


def select(source, position):
    return jnp.take(source, position, axis=1)


def forward_blocks(rows_in, values):
    return jnp.einsum("tsk,skn->tsn", rows_in, values, preferred_element_type=jnp.float32)


def backward_blocks(rows_in, values):
    return jnp.einsum("tsn,skn->tsk", rows_in, values, preferred_element_type=jnp.float32)


def slot_term(left, right, weight):
    product = jnp.einsum("tsk,tsn->skn", left, right, preferred_element_type=jnp.float32)
    return product * weight[:, None, None]


def body(
    tokens, grad_out, gate_blocks, gate_values, up_blocks, up_values, down_blocks, down_values
):
    gathered_x, gathered_dy = (
        lax.all_gather(tokens, "tensor", axis=1, tiled=True),
        lax.all_gather(grad_out, "tensor", axis=1, tiled=True),
    )
    tok_rows, feature_width = gathered_x.shape
    block_size = gate_values.shape[-1]
    feature_count = feature_width // block_size
    hidden_count = FF // (block_size * lax.axis_size("tensor"))
    inputs = gathered_x.reshape(tok_rows, feature_count, block_size)
    upstream = gathered_dy.reshape(tok_rows, feature_count, block_size)
    gate_hid, gate_feat, gate_live = locate(gate_blocks, feature_count)
    up_hid, up_feat, up_live = locate(up_blocks, feature_count)
    down_hid, down_feat, down_live = locate(down_blocks, feature_count)
    gate_rows = select(inputs, gate_feat)
    up_rows = select(inputs, up_feat)
    gate_pre = spread(
        forward_blocks(gate_rows, gate_values[0]), one_hot(gate_hid, gate_live, hidden_count)
    )
    up_pre = spread(forward_blocks(up_rows, up_values[0]), one_hot(up_hid, up_live, hidden_count))
    sigma_gate = jax.nn.sigmoid(gate_pre)
    activated = gate_pre * sigma_gate
    hidden = (activated * up_pre).astype(jnp.bfloat16)
    hidden_rows = select(hidden, down_hid)
    mixed_part = spread(
        forward_blocks(hidden_rows, down_values[0]), one_hot(down_feat, down_live, feature_count)
    )
    mixed_part = mixed_part.reshape(tok_rows, feature_width)
    upstream_rows = select(upstream, down_feat)
    mixed = lax.psum_scatter(
        mixed_part.astype(jnp.bfloat16), "tensor", scatter_dimension=1, tiled=True
    )
    hidden_grad = spread(
        backward_blocks(upstream_rows, down_values[0]), one_hot(down_hid, down_live, hidden_count)
    )
    gate_delta = (hidden_grad * up_pre * sigma_gate * (1.0 + gate_pre * (1.0 - sigma_gate))).astype(
        jnp.bfloat16
    )
    up_delta = (hidden_grad * activated).astype(jnp.bfloat16)
    gate_delta_rows = select(gate_delta, gate_hid)
    up_delta_rows = select(up_delta, up_hid)
    input_part = spread(
        backward_blocks(gate_delta_rows, gate_values[0]),
        one_hot(gate_feat, gate_live, feature_count),
    )
    input_part = input_part + spread(
        backward_blocks(up_delta_rows, up_values[0]), one_hot(up_feat, up_live, feature_count)
    )
    input_part = input_part.reshape(tok_rows, feature_width)
    gate_term = slot_term(gate_rows, gate_delta_rows, gate_live)
    up_term = slot_term(up_rows, up_delta_rows, up_live)
    down_term = slot_term(hidden_rows, upstream_rows, down_live)
    combined = lax.psum_scatter(
        jnp.stack([gate_term, up_term, down_term], axis=1).astype(jnp.bfloat16),
        "dp",
        scatter_dimension=0,
        tiled=True,
    ).astype(jnp.float32)
    grad_gate = combined[None, :, 0]
    grad_up = combined[None, :, 1]
    grad_down = combined[None, :, 2]
    grad_tokens = lax.psum_scatter(
        input_part.astype(jnp.bfloat16), "tensor", scatter_dimension=1, tiled=True
    )
    return (mixed, grad_tokens, grad_gate, grad_up, grad_down)


def solution(mesh):
    in_specs = (
        P("dp", "tensor"),
        P("dp", "tensor"),
        P("tensor", None),
        P("tensor", None, None, None),
        P("tensor", None),
        P("tensor", None, None, None),
        P("tensor", None),
        P("tensor", None, None, None),
    )
    out_specs = (
        P("dp", "tensor"),
        P("dp", "tensor"),
        P("tensor", "dp", None, None),
        P("tensor", "dp", None, None),
        P("tensor", "dp", None, None),
    )
    return jax.shard_map(body, mesh=mesh, in_specs=in_specs, out_specs=out_specs, check_vma=False)
```

profile of v0, /device:TPU:8, one launch (start us, length us, event | category | flops | bytes accessed | tf_op | source)
XLA Modules:
  0.0 338.6 jit_solution(3957242304848105937)
XLA Ops:
  7.2 1.7 copy.68
  9.0 1.7 copy.76
  14.9 24.2 %all-gather.3.cloned.1.call-done = bf16[128,4096]{0,1:T(8,128)(2,1)} async-done(((bf16[128,512]{0,1:T(8,128)(2,1)}), bf16[128,4096]{0,1:T(8,128)(2,1)}) %all-gather.3.cloned.1.call-update) | async-done | bytes 1048592 | tf_op jit(solution)/shard_map/all_gather | solution.py:45
  39.1 1.6 copy.69
  40.7 1.7 gather_fusion
  42.4 1.7 gather_fusion.1
  44.0 23.2 %all-gather.5.cloned.1.call-done = bf16[128,4096]{0,1:T(8,128)(2,1)} async-done(((bf16[128,512]{0,1:T(8,128)(2,1)}), bf16[128,4096]{0,1:T(8,128)(2,1)}) %all-gather.5.cloned.1.call-update) | async-done | bytes 1048592 | tf_op jit(solution)/shard_map/all_gather | solution.py:46
  67.2 2.3 copy.77
  70.0 3.2 fusion.10
  73.8 3.3 fusion.8
  77.0 2.9 gather_fusion.3
  79.9 2.1 convolution_bitcast_fusion.2
  82.0 2.2 fusion.4
  84.3 1.1 fusion.40
  85.4 1.7 gather_fusion.4
  87.0 3.2 fusion.17
  90.2 1.7 gather_fusion.5
  91.9 3.2 fusion.18
  95.1 1.7 gather_fusion.2
  96.8 2.5 fusion.19
  99.4 2.0 pad_maximum_fusion
  101.5 2.2 convolution_bitcast_fusion
  103.7 0.9 convolution_bitcast_fusion.1
  104.6 3.0 fusion
  107.6 3.1 add_convert_fusion
  110.8 1.4 copy.123
  113.2 3.0 fusion.14
  116.2 1.5 copy.124
  118.4 140.7 %all-reduce.3.cloned.1.call-done = bf16[32,3,128,128]{3,2,0,1:T(8,128)(2,1)} async-done(((bf16[32,3,128,128]{3,2,0,1:T(8,128)(2,1)}), bf16[32,3,128,128]{3,2,0,1:T(8,128)(2,1)}) %all-reduce.3.cloned.1.call-update) | async-done | bytes 3145744
  259.0 1.6 dynamic-slice_convert_fusion
  261.3 34.3 %reduce-scatter.8.cloned.1.call-done = bf16[128,512]{1,0:T(8,128)(2,1)} async-done(((bf16[128,4096]{1,0:T(8,128)(2,1)}), bf16[128,512]{1,0:T(8,128)(2,1)}) %reduce-scatter.8.cloned.1.call-update) | async-done | bytes 131088 | tf_op jit(solution)/shard_map/reduce_scatter | solution.py:104
  295.5 36.6 %reduce-scatter.6.cloned.1.call-done = bf16[128,512]{1,0:T(8,128)(2,1)} async-done(((bf16[128,4096]{1,0:T(8,128)(2,1)}), bf16[128,512]{1,0:T(8,128)(2,1)}) %reduce-scatter.6.cloned.1.call-update) | async-done | bytes 131088 | tf_op jit(solution)/shard_map/reduce_scatter | solution.py:72
  (59 shorter events, 7.6 us)
Async XLA Ops:
  7.2 66.1 %copy-start = (bf16[1,32,128,128]{3,2,1,0:T(8,128)(2,1)S(1)}, bf16[1,32,128,128]{3,2,1,0:T(8,128)(2,1)}, u32[]{:S(2)}) copy-start(bf16[1,32,128,128]{3,2,1,0:T(8,128)(2,1)} %param.17) | copy-start | bytes 3145732
  7.2 31.9 %all-gather.3.cloned.1.call-start = ((), (), s32[]{:S(2)}) async-start(), calls=%async_computation.2 | async-start | bytes 1179648 | tf_op jit(solution)/shard_map/all_gather | solution.py:45
  9.0 58.3 %all-gather.5.cloned.1.call-start = ((), (), s32[]{:S(2)}) async-start(), calls=%async_computation.4 | async-start | bytes 1179648 | tf_op jit(solution)/shard_map/all_gather | solution.py:46
  10.7 248.3 %all-reduce.3.cloned.1.call-start = ((), (), s32[]{:S(2)}) async-start(), calls=%async_computation.6 | async-start | bytes 6291456
  42.4 27.1 %copy-start.1 = (bf16[1,32,128,128]{3,2,1,0:T(8,128)(2,1)S(1)}, bf16[1,32,128,128]{3,2,1,0:T(8,128)(2,1)}, u32[]{:S(2)}) copy-start(bf16[1,32,128,128]{3,2,1,0:T(8,128)(2,1)} %param.15) | copy-start | bytes 3145732
  44.0 25.5 %copy-start.7 = (bf16[32,128,128]{2,1,0:T(8,128)(2,1)S(1)}, bf16[32,128,128]{2,1,0:T(8,128)(2,1)}, u32[]{:S(2)}) copy-start(bf16[32,128,128]{2,1,0:T(8,128)(2,1)} %gather_fusion) | copy-start | bytes 3145732
  70.0 3.2 copy-start.5
  73.7 6.2 %copy-start.2 = (bf16[1,32,128,128]{3,2,1,0:T(8,128)(2,1)S(1)}, bf16[1,32,128,128]{3,2,1,0:T(8,128)(2,1)}, u32[]{:S(2)}) copy-start(bf16[1,32,128,128]{3,2,1,0:T(8,128)(2,1)} %param.19) | copy-start | bytes 3145732
  82.0 2.3 copy-start.8
  82.0 2.3 copy-start.9
  96.8 2.5 copy-start.10
  96.8 2.6 copy-start.11
  101.5 2.3 copy-start.6
  101.5 194.1 %reduce-scatter.8.cloned.1.call-start = ((), (), s32[]{:S(2)}) async-start(), calls=%async_computation.5 | async-start | bytes 1179648 | tf_op jit(solution)/shard_map/reduce_scatter | solution.py:104
  110.8 1.7 copy-start.3
  110.8 1.9 copy-start.4
  112.2 219.9 %reduce-scatter.6.cloned.1.call-start = ((), (), s32[]{:S(2)}) async-start(), calls=%async_computation.3 | async-start | bytes 1179648 | tf_op jit(solution)/shard_map/reduce_scatter | solution.py:72
  116.2 1.5 copy-start.12
Sparse Core Ops, SparseCore 0:
  10.4 28.6 all-gather.2
  41.5 25.6 all-gather.4
  101.6 157.3 all-reduce.2
  262.0 33.5 reduce-scatter.7
  298.5 33.5 reduce-scatter.5
where the time goes:
time: 339 us
  waiting for transfers between devices  259 us (76%)
  matrix products  33.4 us (10%)
  local copies, waits for them, and re-layouts  23 us (7%)
  between operations  14.1 us (4%)
  other arithmetic  8.69 us (3%)
    unnamed x6, waiting for transfers between devices  141 us
    reduce_scatter x1, waiting for transfers between devices, body(): lax.psum_scatter(mixed_part.astype(jnp.bfloat16), 'tensor', scatter_dimen...  36.6 us
    reduce_scatter x1, waiting for transfers between devices, body(): lax.psum_scatter(input_part.astype(jnp.bfloat16), 'tensor', scatter_dimen...  34.3 us
    all_gather x1, waiting for transfers between devices, body(): lax.all_gather(tokens, 'tensor', axis=1, tiled=True)  24.2 us
    all_gather x1, waiting for transfers between devices, body(): lax.all_gather(grad_out, 'tensor', axis=1, tiled=True)  23.2 us
    dot_general x6, matrix products, spread(): jnp.einsum('tsn,sc->tcn', product, table, precision=lax.Precision.HIGHEST)  17.9 us
    gather x6, local copies, waits for them, and re-layouts, select(): return jnp.take(source, position, axis=1)  11.3 us
    dot_general x3, matrix products, slot_term(): jnp.einsum('tsk,tsn->skn', left, right, preferred_element_type=jnp.float32)  8.89 us
  transfers between devices with their start and end apart: 5, of which 5 were waited for; matrix products, arithmetic and copies ran while one was open for 9% of the time, Pallas kernels for 0%

commit v1 on v0

--- a/solution.py
+++ b/solution.py
@@ -43,7 +43,12 @@
 ):
     gathered_x, gathered_dy = (
         lax.all_gather(tokens, "tensor", axis=1, tiled=True),
-        lax.all_gather(grad_out, "tensor", axis=1, tiled=True),
+        jnp.concatenate(
+            lax.all_to_all(
+                jnp.stack([grad_out for _ in range(lax.axis_size("tensor"))]), "tensor", 0, 0
+            ),
+            axis=1,
+        ),
     )
     tok_rows, feature_width = gathered_x.shape
     block_size = gate_values.shape[-1]

time: 339 us -> 310 us (0.914)
  waiting for transfers between devices: 259 us -> 231 us
  starting transfers between devices: 0.43 us -> 4.68 us
  other arithmetic: 8.69 us -> 4.73 us
    all_gather x1, waiting for transfers between devices: 24.2 us -> 0.01 us  [body(): lax.all_gather(tokens, 'tensor', axis=1, tiled=True)]
    all_gather x1 -> x0, waiting for transfers between devices: 23.2 us -> none  [body(): lax.all_gather(grad_out, 'tensor', axis=1, tiled=True)]
    all_to_all x0 -> x1, waiting for transfers between devices: none -> 17.7 us  [body(): lax.all_to_all(jnp.stack([grad_out for _ in range(lax.axis_size('tensor')...]
    all_to_all x0 -> x1, starting transfers between devices: none -> 4.3 us  [body(): lax.all_to_all(jnp.stack([grad_out for _ in range(lax.axis_size('tensor')...]
    unnamed x6 -> x5, waiting for transfers between devices: 141 us -> 142 us
    unnamed x32 -> x36, local copies, waits for them, and re-layouts: 7.85 us -> 7.51 us
  transfers between devices with their start and end apart: 5 -> 5, of which waited for: 5 -> 4; matrix products, arithmetic and copies ran while one was open for 9% -> 9% of each run, Pallas kernels for 0% -> 0%
where the time goes in v1:
time: 310 us; the launch traced here: 309 us
  waiting for transfers between devices  231 us (75%)
  matrix products  32.1 us (10%)
  local copies, waits for them, and re-layouts  22.3 us (7%)
  between operations  14.2 us (5%)
  other arithmetic  4.73 us (2%)
  starting transfers between devices  4.68 us (2%)
    unnamed x5, waiting for transfers between devices  142 us
    reduce_scatter x1, waiting for transfers between devices, body(): lax.psum_scatter(mixed_part.astype(jnp.bfloat16), 'tensor', scatter_dimen...  36.6 us
    reduce_scatter x1, waiting for transfers between devices, body(): lax.psum_scatter(input_part.astype(jnp.bfloat16), 'tensor', scatter_dimen...  34.4 us
    all_to_all x1, waiting for transfers between devices, body(): lax.all_to_all(jnp.stack([grad_out for _ in range(lax.axis_size('tensor')...  17.7 us
    dot_general x6, matrix products, spread(): jnp.einsum('tsn,sc->tcn', product, table, precision=lax.Precision.HIGHEST)  16.8 us
    gather x6, local copies, waits for them, and re-layouts, select(): return jnp.take(source, position, axis=1)  10.6 us
    dot_general x3, matrix products, slot_term(): jnp.einsum('tsk,tsn->skn', left, right, preferred_element_type=jnp.float32)  8.72 us
    unnamed x36, local copies, waits for them, and re-layouts  7.51 us
  transfers between devices with their start and end apart: 5, of which 4 were waited for; matrix products, arithmetic and copies ran while one was open for 9% of the time, Pallas kernels for 0%

profile of v1, /device:TPU:8, one launch (start us, length us, event | category | flops | bytes accessed | tf_op | source)
XLA Modules:
  0.0 309.2 jit_solution(8520456577807228322)
XLA Ops:
  7.3 1.7 copy.70
  9.0 1.0 copy.78
  10.0 1.1 stack.27
  11.2 4.3 %all-to-all-start = ((bf16[8,128,512]{1,2,0:T(8,128)(2,1)}), bf16[8,128,512]{1,2,0:T(8,128)(2,1)S(1)}, u32[]{:S(2)}, u32[]{:S(2)}) async-start(bf16[8,128,512]{1,2,0:T(8,128)(2,1)} %stack.27), calls=%async_computation.1 | async-start | bytes 2097152 | tf_op jit(solution)/shard_map/all_to_all | solution.py:47
  15.8 17.7 %all-to-all-done = bf16[8,128,512]{1,2,0:T(8,128)(2,1)S(1)} async-done(((bf16[8,128,512]{1,2,0:T(8,128)(2,1)}), bf16[8,128,512]{1,2,0:T(8,128)(2,1)S(1)}, u32[]{:S(2)}, u32[]{:S(2)}) %all-to-all-start) | async-done | bytes 1048608 | tf_op jit(solution)/shard_map/all_to_all | solution.py:47
  33.5 1.3 copy.79
  34.8 2.0 gather_fusion.3
  37.8 3.2 %fusion.4 = f32[14,128,128]{2,0,1:T(8,128)} fusion(f32[128,32,128]{2,0,1:T(8,128)S(1)} %convolution_bitcast_fusion.2, f32[32]{0:T(128)S(1)} %fusion.80, s32[32]{0:T(128)S(1)} %get-tuple-element.51), kind=kOutput, calls=%fused_computation.11 | convolution fusion | flops 88081280 | bytes 3014912 | tf_op jit(solution)/shard_map/tsn,sc->tcn/dot_general | solution.py:21
  41.0 1.8 copy.71
  42.8 1.7 gather_fusion
  44.5 1.7 gather_fusion.1
  46.3 1.7 convolution_bitcast_fusion.5
  48.0 2.2 fusion.10
  50.8 2.2 fusion.8
  53.0 1.1 fusion.40
  54.1 1.7 gather_fusion.4
  55.7 3.2 %fusion.17 = bf16[32,1,128,128]{3,2,0,1:T(8,128)(2,1)} fusion(f32[32]{0:T(128)S(1)} %fusion.81, bf16[32,128,128]{2,1,0:T(8,128)(2,1)} %gather_fusion, pred[32]{0:T(512)(128)(4,1)S(1)} %get-tuple-element.52, bf16[32,128,128]{2,1,0:T(8,128)(2,1)} %gather_fusion.4, pred[32]{0:T(512)(128)(4,1)S(1)} %get-tuple-element.32), kind=kOutput, calls=%fused_computation.30 | convolution fusion | flops 136314880 | bytes 3145920 | tf_op jit(solution)/shard_map/tsk,tsn->skn/dot_general | solution.py:37
  58.9 1.8 gather_fusion.5
  60.7 3.2 %fusion.18 = bf16[32,1,128,128]{3,2,0,1:T(8,128)(2,1)} fusion(f32[32]{0:T(128)S(1)} %fusion.82, bf16[32,128,128]{2,1,0:T(8,128)(2,1)} %gather_fusion.1, pred[32]{0:T(512)(128)(4,1)S(1)} %get-tuple-element.54, bf16[32,128,128]{2,1,0:T(8,128)(2,1)} %gather_fusion.5, pred[32]{0:T(512)(128)(4,1)S(1)} %get-tuple-element.34), kind=kOutput, calls=%fused_computation.31 | convolution fusion | flops 136314880 | bytes 3145920 | tf_op jit(solution)/shard_map/tsk,tsn->skn/dot_general | solution.py:37
  63.9 1.7 gather_fusion.2
  65.6 2.4 fusion.19
  68.0 2.0 pad_maximum_fusion
  70.3 2.1 convolution_bitcast_fusion
  73.4 3.0 fusion
  76.4 3.1 %add_convert_fusion = bf16[32,128,128]{2,0,1:T(8,128)(2,1)S(1)} fusion(f32[32,128,128]{2,0,1:T(8,128)S(1)} %fusion, f32[128,32,128]{2,0,1:T(8,128)S(1)} %convolution_bitcast_fusion.1, f32[32]{0:T(128)S(1)} %fusion.81, s32[32]{0:T(128)S(1)} %get-tuple-element.53), kind=kOutput, calls=%fused_computation.22 | convolution fusion | flops 202377216 | bytes 5243136 | tf_op jit(solution)/shard_map/tsn,sc->tcn/dot_general | solution.py:21
  79.5 1.4 copy.125
  81.9 3.0 fusion.14
  84.9 1.5 copy.126
  87.1 142.3 %all-reduce.3.cloned.1.call-done = bf16[32,3,128,128]{3,2,0,1:T(8,128)(2,1)} async-done(((bf16[32,3,128,128]{3,2,0,1:T(8,128)(2,1)}), bf16[32,3,128,128]{3,2,0,1:T(8,128)(2,1)}) %all-reduce.3.cloned.1.call-update) | async-done | bytes 3145744
  229.4 1.6 dynamic-slice_convert_fusion
  231.7 34.4 %reduce-scatter.8.cloned.1.call-done = bf16[128,512]{1,0:T(8,128)(2,1)} async-done(((bf16[128,4096]{1,0:T(8,128)(2,1)}), bf16[128,512]{1,0:T(8,128)(2,1)}) %reduce-scatter.8.cloned.1.call-update) | async-done | bytes 131088 | tf_op jit(solution)/shard_map/reduce_scatter | solution.py:109
  266.1 36.6 %reduce-scatter.6.cloned.1.call-done = bf16[128,512]{1,0:T(8,128)(2,1)} async-done(((bf16[128,4096]{1,0:T(8,128)(2,1)}), bf16[128,512]{1,0:T(8,128)(2,1)}) %reduce-scatter.6.cloned.1.call-update) | async-done | bytes 131088 | tf_op jit(solution)/shard_map/reduce_scatter | solution.py:77
  (63 shorter events, 5.1 us)
Async XLA Ops:
  7.2 43.1 %copy-start = (bf16[1,32,128,128]{3,2,1,0:T(8,128)(2,1)S(1)}, bf16[1,32,128,128]{3,2,1,0:T(8,128)(2,1)}, u32[]{:S(2)}) copy-start(bf16[1,32,128,128]{3,2,1,0:T(8,128)(2,1)} %param.17) | copy-start | bytes 3145732
  7.2 8.4 %copy-start.11 = (s32[1,32]{1,0:T(1,128)S(1)}, s32[1,32]{1,0:T(1,128)}, u32[]{:S(2)}) copy-start(s32[1,32]{1,0:T(1,128)} %param.14) | copy-start | bytes 388
  7.2 8.4 %copy-start.12 = (s32[1,32]{1,0:T(1,128)S(1)}, s32[1,32]{1,0:T(1,128)}, u32[]{:S(2)}) copy-start(s32[1,32]{1,0:T(1,128)} %param.16) | copy-start | bytes 388
  7.2 8.5 %copy-start.13 = (s32[1,32]{1,0:T(1,128)S(1)}, s32[1,32]{1,0:T(1,128)}, u32[]{:S(2)}) copy-start(s32[1,32]{1,0:T(1,128)} %param.18) | copy-start | bytes 388
  7.2 33.8 %all-gather.2.cloned.1.call-start = ((), (), s32[]{:S(2)}) async-start(), calls=%async_computation.3 | async-start | bytes 1179648 | tf_op jit(solution)/shard_map/all_gather | solution.py:45
  11.2 22.3 %all-to-all-start = ((bf16[8,128,512]{1,2,0:T(8,128)(2,1)}), bf16[8,128,512]{1,2,0:T(8,128)(2,1)S(1)}, u32[]{:S(2)}, u32[]{:S(2)}) async-start(bf16[8,128,512]{1,2,0:T(8,128)(2,1)} %stack.27), calls=%async_computation.1 | async-start | bytes 2097152 | tf_op jit(solution)/shard_map/all_to_all | solution.py:47
  15.5 213.9 %all-reduce.3.cloned.1.call-start = ((), (), s32[]{:S(2)}) async-start(), calls=%async_computation.6 | async-start | bytes 6291456
  33.5 3.3 %copy-start.2 = (bf16[1,32,128,128]{3,2,1,0:T(8,128)(2,1)S(1)}, bf16[1,32,128,128]{3,2,1,0:T(8,128)(2,1)}, u32[]{:S(2)}) copy-start(bf16[1,32,128,128]{3,2,1,0:T(8,128)(2,1)} %param.19) | copy-start | bytes 3145732
  36.8 1.0 copy-start.4
  42.8 3.4 %copy-start.1 = (bf16[1,32,128,128]{3,2,1,0:T(8,128)(2,1)S(1)}, bf16[1,32,128,128]{3,2,1,0:T(8,128)(2,1)}, u32[]{:S(2)}) copy-start(bf16[1,32,128,128]{3,2,1,0:T(8,128)(2,1)} %param.15) | copy-start | bytes 3145732
  48.0 2.3 copy-start.7
  50.8 2.3 copy-start.8
  65.6 2.4 copy-start.9
  65.6 2.4 copy-start.10
  70.0 2.4 copy-start.6
  70.0 196.0 %reduce-scatter.8.cloned.1.call-start = ((), (), s32[]{:S(2)}) async-start(), calls=%async_computation.5 | async-start | bytes 1179648 | tf_op jit(solution)/shard_map/reduce_scatter | solution.py:109
  79.5 1.5 copy-start.3
  79.5 1.9 copy-start.5
  81.0 221.7 %reduce-scatter.6.cloned.1.call-start = ((), (), s32[]{:S(2)}) async-start(), calls=%async_computation.4 | async-start | bytes 1179648 | tf_op jit(solution)/shard_map/reduce_scatter | solution.py:77
  84.9 1.6 copy-start.14
Sparse Core Ops, SparseCore 0:
  10.5 30.0 all-gather.1
  70.2 159.2 all-reduce.2
  232.5 33.5 reduce-scatter.7
  269.0 33.5 reduce-scatter.5
